TPU v7x, 32 devices: a whole 2x2x4 slice. The times are simulated.
32 devices in a mesh: groups: 2 (over y), seq: 8 (over z, x), wg: 2 (over core).
Axes of the slice: x: 2, y: 2, z: 4, core: 2. Of those that a mesh axis runs over, the one named last changes fastest.
Arguments:
- generator_rows: bfloat16 [2048, 2304], P(('groups', 'seq'), 'wg'), parts along dimension 0, may hold values from -120 to 120, as said below
- pre_gain: float32 [2304], replicated, may hold values from 0.1 to 1.9
- query_weight: bfloat16 [2304, 2048], P('seq', 'wg'), may hold values from -2 to 2, as said below
- key_weight: bfloat16 [2304, 1024], P('seq', 'wg'), may hold values from -2 to 2, as said below
- value_weight: bfloat16 [2304, 1024], P('seq', 'wg'), may hold values from -0.125 to 0.125
- out_weight: bfloat16 [2048, 2304], P('wg', 'seq'), may hold values from -0.125 to 0.125
- post_gain: float32 [2304], replicated, may hold values from 0.1 to 1.9
- final_gain: float32 [2304], replicated, may hold values from 0.1 to 1.9
- label_table: bfloat16 [64, 2304], replicated, may hold values from -0.375 to 0.375
- lengths: int32 [16], P('groups'), parts along dimension 0, may hold values from 65 to 127
- label_index: int32 [16], P('groups'), parts along dimension 0, may hold values from 0 to 63
Outputs:
- input_grad: bfloat16 [2048, 2304], P(('groups', 'seq'), 'wg'), parts along dimension 0
There are 2 independent parts, one for each index of `groups`. A program takes and returns all parts, laid end to end along the dimension named above; an argument that names none is the same for every part. Nothing has to cross between parts.
Inputs may be any that keep to these rules, and one draw needn't show every extreme that they name: `generator_rows`: finite real entries. `query_weight`: finite real entries. `key_weight`: finite real entries.
All inputs are finite; a program needn't handle non-finite values.
Results may differ from a plain program's by a relative error of at most 0.017.
The roundings to bfloat16 on the way count: a program that leaves them out, or rounds other values in their place, can miss the bound.
Values may be sent and summed in bfloat16 or wider, within the bound.
No kernel may reach another device: no remote copies, remote signals or barrier semaphores. Data moves between devices by JAX's collectives and lax.ppermute only.
A program may use at most 128 MiB of HBM per device.

v0:
```python
import jax
import jax.numpy as jnp
from jax import lax
from jax.sharding import PartitionSpec as P

HD = 128
LABELS = 64
EPSILON = 1e-06
ATTEND_CAP = 50.0
LABEL_CAP = 30.0
QUERY_SCALE = 1.0 / 12.0


def rope_tables(positions, head_width):
    frequency = 10000.0 ** (-2.0 * jnp.arange(head_width // 2, dtype=jnp.float32) / head_width)
    angles = positions.astype(jnp.float32)[:, None] * frequency[None, :]
    return (jnp.cos(angles), jnp.sin(angles))


def rotate(values, cos_table, sin_table):
    half_width = values.shape[-1] // 2
    lower_part = values[..., :half_width]
    upper_part = values[..., half_width:]
    return jnp.concatenate(
        [
            lower_part * cos_table - upper_part * sin_table,
            upper_part * cos_table + lower_part * sin_table,
        ],
        axis=-1,
    )


def rotate_back(values, cos_table, sin_table):
    half_width = values.shape[-1] // 2
    lower_part = values[..., :half_width]
    upper_part = values[..., half_width:]
    return jnp.concatenate(
        [
            lower_part * cos_table + upper_part * sin_table,
            upper_part * cos_table - lower_part * sin_table,
        ],
        axis=-1,
    )


def times_transposed(left_side, right_side):
    return lax.dot_general(
        left_side, right_side, (((1,), (1,)), ((), ())), preferred_element_type=jnp.float32
    )


def shards(
    generator_rows,
    pre_gain,
    query_weight,
    key_weight,
    value_weight,
    out_weight,
    post_gain,
    final_gain,
    label_table,
    lengths,
    label_index,
):
    seq_rank = lax.axis_index("seq")
    core_rank = lax.axis_index("wg")
    whole_rows = lax.all_gather(generator_rows, "wg", axis=1, tiled=True)
    guard_rows = lax.all_to_all(whole_rows, "seq", split_axis=0, concat_axis=0, tiled=True)
    w_query, w_key, w_value, w_out = (
        lax.all_gather(query_weight, "seq", axis=0, tiled=True),
        lax.all_gather(key_weight, "seq", axis=0, tiled=True),
        lax.all_gather(value_weight, "seq", axis=0, tiled=True),
        lax.all_gather(out_weight, "seq", axis=1, tiled=True),
    )
    tok_rows = guard_rows.shape[0]
    half_width = generator_rows.shape[1]
    local_heads = w_query.shape[1] // HD
    local_kv = w_key.shape[1] // HD
    group_size = local_heads // local_kv
    length = lax.dynamic_index_in_dim(lengths, seq_rank, 0, keepdims=False)
    target = lax.dynamic_index_in_dim(label_index, seq_rank, 0, keepdims=False)
    offsets = jnp.arange(tok_rows, dtype=jnp.int32)
    cos_table, sin_table = rope_tables(offsets, HD)
    inputs = guard_rows.astype(jnp.float32)
    scale_in = lax.rsqrt(jnp.mean(inputs * inputs, axis=-1, keepdims=True) + EPSILON)
    normed = (inputs * scale_in * pre_gain).astype(jnp.bfloat16)
    query_proj = (
        jnp.dot(normed, w_query, preferred_element_type=jnp.float32)
        .reshape(tok_rows, local_heads, HD)
        .transpose(1, 0, 2)
    )
    queries = (rotate(query_proj, cos_table, sin_table) * QUERY_SCALE).astype(jnp.bfloat16)
    key_proj = (
        jnp.dot(normed, w_key, preferred_element_type=jnp.float32)
        .reshape(tok_rows, local_kv, HD)
        .transpose(1, 0, 2)
    )
    keys_own = rotate(key_proj, cos_table, sin_table).astype(jnp.bfloat16)
    values_own = (
        jnp.dot(normed, w_value, preferred_element_type=jnp.float32)
        .astype(jnp.bfloat16)
        .reshape(tok_rows, local_kv, HD)
        .transpose(1, 0, 2)
    )
    allowed = (offsets[None, :] <= offsets[:, None]) & (offsets[None, :] < length)
    query_four = queries.reshape(local_kv, group_size, tok_rows, HD)
    raw_scores = jnp.einsum(
        "kgid,kjd->kgij", query_four, keys_own, preferred_element_type=jnp.float32
    )
    capped = jnp.tanh(raw_scores / ATTEND_CAP)
    weight_exp = jnp.where(allowed[None, None], jnp.exp(ATTEND_CAP * capped), 0.0)
    soft_weights = weight_exp / jnp.sum(weight_exp, axis=-1, keepdims=True)
    attend = soft_weights.astype(jnp.bfloat16)
    context = jnp.einsum(
        "kgij,kjd->kgid", attend, values_own, preferred_element_type=jnp.float32
    ).astype(jnp.bfloat16)
    context_rows = (
        context.reshape(local_heads, tok_rows, HD)
        .transpose(1, 0, 2)
        .reshape(tok_rows, local_heads * HD)
    )
    out_part = jnp.dot(context_rows, w_out, preferred_element_type=jnp.float32)
    attention = lax.psum(out_part.astype(jnp.bfloat16), "wg").astype(jnp.float32)
    scale_attn = lax.rsqrt(jnp.mean(attention * attention, axis=-1, keepdims=True) + EPSILON)
    mixed_rows = inputs + attention * scale_attn * post_gain
    scale_out = lax.rsqrt(jnp.mean(mixed_rows * mixed_rows, axis=-1, keepdims=True) + EPSILON)
    final_rows = (mixed_rows * scale_out * final_gain).astype(jnp.bfloat16)
    logits = times_transposed(final_rows, label_table)
    label_cap = jnp.tanh(logits / LABEL_CAP)
    label_exp = jnp.exp(LABEL_CAP * label_cap)
    chance = label_exp / jnp.sum(label_exp, axis=-1, keepdims=True)
    live_rows = (offsets < length)[:, None]
    onehot = (jnp.arange(LABELS, dtype=jnp.int32) == target).astype(jnp.float32)[None, :]
    grad_logit = (
        jnp.where(live_rows, chance - onehot, 0.0) * (1.0 - label_cap * label_cap)
    ).astype(jnp.bfloat16)
    grad_final = jnp.dot(grad_logit, label_table, preferred_element_type=jnp.float32)
    scaled_final = grad_final * final_gain
    cube_out = scale_out * scale_out * scale_out
    grad_mixed = scale_out * scaled_final - mixed_rows * cube_out * jnp.mean(
        scaled_final * mixed_rows, axis=-1, keepdims=True
    )
    scaled_post = grad_mixed * post_gain
    cube_attn = scale_attn * scale_attn * scale_attn
    grad_attention = scale_attn * scaled_post - attention * cube_attn * jnp.mean(
        scaled_post * attention, axis=-1, keepdims=True
    )
    grad_context = times_transposed(grad_attention.astype(jnp.bfloat16), w_out).astype(jnp.bfloat16)
    grad_four = grad_context.reshape(tok_rows, local_kv, group_size, HD).transpose(1, 2, 0, 3)
    grad_prob = jnp.einsum(
        "kgid,kjd->kgij", grad_four, values_own, preferred_element_type=jnp.float32
    )
    grad_score = (
        soft_weights
        * (grad_prob - jnp.sum(soft_weights * grad_prob, axis=-1, keepdims=True))
        * (1.0 - capped * capped)
    )
    score_round = grad_score.astype(jnp.bfloat16)
    grad_query = jnp.einsum(
        "kgij,kjd->kgid", score_round, keys_own, preferred_element_type=jnp.float32
    ).reshape(local_heads, tok_rows, HD)
    grad_queries = rotate_back(grad_query * QUERY_SCALE, cos_table, sin_table).astype(jnp.bfloat16)
    grad_key = jnp.einsum(
        "kgij,kgid->kjd", score_round, query_four, preferred_element_type=jnp.float32
    )
    grad_value = jnp.einsum("kgij,kgid->kjd", attend, grad_four, preferred_element_type=jnp.float32)
    grad_keys = rotate_back(grad_key, cos_table, sin_table).astype(jnp.bfloat16)
    grad_values = grad_value.astype(jnp.bfloat16)
    query_rows = grad_queries.transpose(1, 0, 2).reshape(tok_rows, local_heads * HD)
    key_rows = grad_keys.transpose(1, 0, 2).reshape(tok_rows, local_kv * HD)
    value_rows = grad_values.transpose(1, 0, 2).reshape(tok_rows, local_kv * HD)
    grad_part = (
        times_transposed(query_rows, w_query)
        + times_transposed(key_rows, w_key)
        + times_transposed(value_rows, w_value)
    )
    cube_in = scale_in * scale_in * scale_in
    grad_normed = lax.psum(grad_part.astype(jnp.bfloat16), "wg").astype(jnp.float32)
    scaled_in = grad_normed * pre_gain
    row_stat = jnp.mean(scaled_in * inputs, axis=-1, keepdims=True)
    grad_full = scale_in * scaled_in - inputs * cube_in * row_stat + grad_mixed
    grad_rows = lax.dynamic_slice_in_dim(grad_full, core_rank * half_width, half_width, 1)
    return lax.all_to_all(
        grad_rows.astype(jnp.bfloat16), "seq", split_axis=0, concat_axis=0, tiled=True
    )


def solution(mesh):
    return jax.shard_map(
        shards,
        mesh=mesh,
        in_specs=(
            P(("groups", "seq"), "wg"),
            P(),
            P("seq", "wg"),
            P("seq", "wg"),
            P("seq", "wg"),
            P("wg", "seq"),
            P(),
            P(),
            P(),
            P("groups"),
            P("groups"),
        ),
        out_specs=P(("groups", "seq"), "wg"),
        check_vma=False,
    )
```

profile of v0, /device:TPU:0, one launch (start us, length us, event | category | flops | bytes accessed | tf_op | source)
XLA Modules:
  0.0 376.7 jit_solution(12886535654456239035)
XLA Ops:
  9.4 2.4 all_gather.15
  11.8 7.2 %all-to-all-start = ((bf16[8,16,2304]{2,1,0:T(8,128)(2,1)}), bf16[8,16,2304]{2,1,0:T(8,128)(2,1)S(1)}, u32[]{:S(2)}, u32[]{:S(2)}) async-start(bf16[8,16,2304]{2,1,0:T(8,128)(2,1)} %bitcast), calls=%async_computation | async-start | bytes 1179648 | tf_op jit(solution)/shard_map/all_to_all | solution.py:68
  20.6 24.1 %all-to-all-done = bf16[8,16,2304]{2,1,0:T(8,128)(2,1)S(1)} async-done(((bf16[8,16,2304]{2,1,0:T(8,128)(2,1)}), bf16[8,16,2304]{2,1,0:T(8,128)(2,1)S(1)}, u32[]{:S(2)}, u32[]{:S(2)}) %all-to-all-start) | async-done | bytes 589856 | tf_op jit(solution)/shard_map/all_to_all | solution.py:68
  44.9 1.0 multiply_convert_fusion.2
  46.0 1.2 bitcast_convert_fusion
  47.1 25.5 %all-gather.7.cloned.1.call-done = bf16[2304,512]{1,0:T(8,128)(2,1)} async-done(((bf16[288,512]{1,0:T(8,128)(2,1)}), bf16[2304,512]{1,0:T(8,128)(2,1)}) %all-gather.7.cloned.1.call-update) | async-done | bytes 2359312 | tf_op jit(solution)/shard_map/all_gather | solution.py:71
  72.7 2.8 copy.15
  75.5 50.0 %all-gather.9.cloned.1.call-done = bf16[2304,512]{1,0:T(8,128)(2,1)} async-done(((bf16[288,512]{1,0:T(8,128)(2,1)}), bf16[2304,512]{1,0:T(8,128)(2,1)}) %all-gather.9.cloned.1.call-update) | async-done | bytes 2359312 | tf_op jit(solution)/shard_map/all_gather | solution.py:72
  125.5 2.5 convolution_convert_fusion.3
  128.1 0.7 copy.50
  128.8 1.8 convolution_bitcast_fusion.3
  130.7 75.5 %all-gather.5.cloned.1.call-done = bf16[2304,1024]{1,0:T(8,128)(2,1)} async-done(((bf16[288,1024]{1,0:T(8,128)(2,1)}), bf16[2304,1024]{1,0:T(8,128)(2,1)}) %all-gather.5.cloned.1.call-update) | async-done | bytes 4718608 | tf_op jit(solution)/shard_map/all_gather | solution.py:70
  206.1 6.8 %copy.12 = bf16[1024,2304]{1,0:T(8,128)(2,1)} copy(bf16[1024,2304]{0,1:T(8,128)(2,1)} %bitcast.103) | data formatting | bytes 9437184 | tf_op jit(solution)/shard_map/dot_general | solution.py:88
  213.0 4.0 %convolution_bitcast_fusion = f32[8,128,128]{1,2,0:T(8,128)S(1)} fusion(bf16[128,2304,1]{1,0,2:T(8,128)(2,1)S(1)} %bitcast.108, bf16[8,128,2304]{2,1,0:T(8,128)(2,1)} %bitcast.104), kind=kOutput, calls=%fused_computation.16 | convolution fusion | flops 603979776 | bytes 5832704 | tf_op jit(solution)/shard_map/dot_general | solution.py:88
  218.9 67.3 %all-gather.11.cloned.1.call-done = bf16[1024,2304]{0,1:T(8,128)(2,1)} async-done(((bf16[1024,288]{0,1:T(8,128)(2,1)}), bf16[1024,2304]{0,1:T(8,128)(2,1)}) %all-gather.11.cloned.1.call-update) | async-done | bytes 4718608 | tf_op jit(solution)/shard_map/all_gather | solution.py:73
  286.3 4.9 %convolution_convert_fusion = bf16[128,2304]{1,0:T(8,128)(2,1)} fusion(bf16[128,1024]{0,1:T(8,128)(2,1)S(1)} %bitcast.118, bf16[1024,2304]{0,1:T(8,128)(2,1)} %all-gather.11.cloned.1.call-done), kind=kOutput, calls=%fused_computation.5 | convolution fusion | flops 604274688 | bytes 5570560 | tf_op jit(solution)/shard_map/dot_general | solution.py:122
  292.7 15.7 %all-reduce.3.cloned.1.call-done = bf16[128,2304]{1,0:T(8,128)(2,1)} async-done(((bf16[128,2304]{1,0:T(8,128)(2,1)}), bf16[128,2304]{1,0:T(8,128)(2,1)}) %all-reduce.3.cloned.1.call-update) | async-done | bytes 589840 | tf_op jit(solution)/shard_map/psum | solution.py:123
  308.3 1.3 fusion.7
  309.6 1.5 multiply_reduce_fusion.2
  312.7 1.3 copy-done.1
  314.0 1.2 convolution_convert_fusion.2
  315.4 2.0 fusion.14
  317.7 1.7 convolution_bitcast_fusion.2
  319.4 2.6 convolution_multiply_fusion.1
  322.0 1.2 copy.24
  323.4 4.2 %fusion.66 = f32[128,2304]{1,0:T(8,128)S(1)} fusion(bf16[128,1024]{0,1:T(8,128)(2,1)S(1)} %bitcast.116, bf16[2304,1024]{1,0:T(8,128)(2,1)} %all-gather.5.cloned.1.call-done), kind=kOutput, calls=%fused_computation.121 | convolution fusion | flops 603979776 | bytes 6160384 | tf_op jit(solution)/shard_map/dot_general | solution.py:47
  327.6 0.9 convolution_add_fusion.1
  328.6 0.7 copy-done.4
  329.3 1.7 fusion.1
  331.1 20.2 %all-reduce.5.cloned.1.call-done = bf16[128,2304]{1,0:T(8,128)(2,1)} async-done(((bf16[128,2304]{1,0:T(8,128)(2,1)}), bf16[128,2304]{1,0:T(8,128)(2,1)}) %all-reduce.5.cloned.1.call-update) | async-done | bytes 589840 | tf_op jit(solution)/shard_map/psum | solution.py:178
  351.2 1.3 multiply_reduce_fusion
  352.8 16.4 %all_to_all.21 = bf16[8,16,1152]{2,1,0:T(8,128)(2,1)S(1)} all-to-all(bf16[8,16,1152]{2,1,0:T(8,128)(2,1)S(1)} %bitcast.110), channel_id=1, replica_groups=mesh['groups'=2,'seq'=8,'wg'=2] {'seq'}, dimensions={0} | all-to-all | bytes 589824 | tf_op jit(solution)/shard_map/all_to_all | solution.py:183
  (89 shorter events, 11.0 us)
Async XLA Ops:
  6.5 304.6 %copy-start = (bf16[64,2304]{1,0:T(8,128)(2,1)S(1)}, bf16[64,2304]{1,0:T(8,128)(2,1)}, u32[]{:S(2)}) copy-start(bf16[64,2304]{1,0:T(8,128)(2,1)} %param.19) | copy-start | bytes 884740
  6.5 2.8 copy-start.7
  6.5 66.1 %all-gather.7.cloned.1.call-start = ((), (), s32[]{:S(2)}) async-start(), calls=%async_computation.3 | async-start | bytes 2654208 | tf_op jit(solution)/shard_map/all_gather | solution.py:71
  7.3 118.2 %all-gather.9.cloned.1.call-start = ((), (), s32[]{:S(2)}) async-start(), calls=%async_computation.4 | async-start | bytes 2654208 | tf_op jit(solution)/shard_map/all_gather | solution.py:72
  8.0 198.1 %all-gather.5.cloned.1.call-start = ((), (), s32[]{:S(2)}) async-start(), calls=%async_computation.2 | async-start | bytes 5308416 | tf_op jit(solution)/shard_map/all_gather | solution.py:70
  8.7 277.5 %all-gather.11.cloned.1.call-start = ((), (), s32[]{:S(2)}) async-start(), calls=%async_computation.5 | async-start | bytes 5308416 | tf_op jit(solution)/shard_map/all_gather | solution.py:73
  9.3 9.7 %copy-start.17 = (s32[8]{0:T(128)S(1)}, s32[8]{0:T(128)}, u32[]{:S(2)}) copy-start(s32[8]{0:T(128)} %param.20) | copy-start | bytes 100
  9.3 35.6 %copy-start.12 = (f32[2304]{0:T(1024)S(1)}, f32[2304]{0:T(1024)}, u32[]{:S(2)}) copy-start(f32[2304]{0:T(1024)} %param.12) | copy-start | bytes 27652
  11.8 32.8 %all-to-all-start = ((bf16[8,16,2304]{2,1,0:T(8,128)(2,1)}), bf16[8,16,2304]{2,1,0:T(8,128)(2,1)S(1)}, u32[]{:S(2)}, u32[]{:S(2)}) async-start(bf16[8,16,2304]{2,1,0:T(8,128)(2,1)} %bitcast), calls=%async_computation | async-start | bytes 1179648 | tf_op jit(solution)/shard_map/all_to_all | solution.py:68
  19.0 289.3 %all-reduce.3.cloned.1.call-start = ((), (), s32[]{:S(2)}) async-start(), calls=%async_computation.6 | async-start | bytes 1179648 | tf_op jit(solution)/shard_map/psum | solution.py:123
  130.7 87.0 %copy-start.14 = (bf16[4,128,64]{1,2,0:T(8,128)(2,1)}, bf16[4,128,64]{1,2,0:T(8,128)(2,1)S(1)}, u32[]{:S(2)}) copy-start(bf16[4,128,64]{1,2,0:T(8,128)(2,1)S(1)} %get-tuple-element.18) | copy-start | bytes 196612
  206.1 6.8 %copy-start.6 = (bf16[8,16,2304]{2,1,0:T(8,128)(2,1)S(1)}, bf16[8,16,2304]{2,1,0:T(8,128)(2,1)}, u32[]{:S(2)}) copy-start(bf16[8,16,2304]{2,1,0:T(8,128)(2,1)} %multiply_convert_fusion.2) | copy-start | bytes 1769476
  217.5 0.9 copy-start.11
  217.7 1.0 copy-start.8
  218.1 0.8 copy-start.19
  218.1 0.8 copy-start.20
  286.3 5.2 %copy-start.18 = (s32[8]{0:T(128)S(1)}, s32[8]{0:T(128)}, u32[]{:S(2)}) copy-start(s32[8]{0:T(128)} %param.21) | copy-start | bytes 100
  291.1 18.4 %copy-start.13 = (f32[2304]{0:T(1024)S(1)}, f32[2304]{0:T(1024)}, u32[]{:S(2)}) copy-start(f32[2304]{0:T(1024)} %param.17) | copy-start | bytes 27652
  291.2 60.1 %all-reduce.5.cloned.1.call-start = ((), (), s32[]{:S(2)}) async-start(), calls=%async_computation.7 | async-start | bytes 1179648 | tf_op jit(solution)/shard_map/psum | solution.py:178
  309.6 1.5 copy-start.16
  311.1 1.1 copy-start.2
  311.6 2.4 copy-start.1
  314.0 1.4 copy-start.21
  315.4 2.2 copy-start.9
  317.7 1.8 copy-start.15
  323.4 4.2 %copy-start.3 = (bf16[2304,512]{1,0:T(8,128)(2,1)S(1)}, bf16[2304,512]{1,0:T(8,128)(2,1)}, u32[]{:S(2)}) copy-start(bf16[2304,512]{1,0:T(8,128)(2,1)} %all-gather.7.cloned.1.call-done) | copy-start | bytes 7077892
  327.6 1.7 copy-start.4
  327.6 1.7 copy-start.10
  331.1 21.5 %copy-start.5 = (f32[128,2304]{1,0:T(8,128)S(1)}, f32[128,2304]{1,0:T(8,128)}, u32[]{:S(2)}) copy-start(f32[128,2304]{1,0:T(8,128)} %bitcast_convert_fusion) | copy-start | bytes 3538948
Sparse Core Ops, SparseCore 0:
  9.5 63.0 all-gather.6
  74.9 50.6 all-gather.8
  127.7 78.4 all-gather.4
  208.2 78.0 all-gather.10
  291.3 16.9 all-reduce.2
  331.2 20.0 all-reduce.4
where the time goes:
time: 378 us; the launch traced here: 377 us
  waiting for transfers between devices  281 us (74%)
  matrix products  29.5 us (8%)
  blocking collectives  18.8 us (5%)
  local copies, waits for them, and re-layouts  16.9 us (4%)
  between operations  13.9 us (4%)
  other arithmetic  9.24 us (2%)
  starting transfers between devices  7.55 us (2%)
    all_gather x1, waiting for transfers between devices, shards(): lax.all_gather(query_weight, 'seq', axis=0, tiled=True)  75.5 us
    all_gather x1, waiting for transfers between devices, shards(): lax.all_gather(out_weight, 'seq', axis=1, tiled=True)  67.3 us
    all_gather x1, waiting for transfers between devices, shards(): lax.all_gather(value_weight, 'seq', axis=0, tiled=True)  50 us
    all_gather x1, waiting for transfers between devices, shards(): lax.all_gather(key_weight, 'seq', axis=0, tiled=True)  25.5 us
    all_to_all x1, waiting for transfers between devices, shards(): lax.all_to_all(whole_rows, 'seq', split_axis=0, concat_axis=0, tiled=True)  24.1 us
    psum x1, waiting for transfers between devices, shards(): lax.psum(grad_part.astype(jnp.bfloat16), 'wg').astype(jnp.float32)  20.2 us
    all_to_all x1, blocking collectives, shards(): lax.all_to_all(grad_rows.astype(jnp.bfloat16), 'seq', split_axis=0, conca...  16.4 us
    psum x1, waiting for transfers between devices, shards(): lax.psum(out_part.astype(jnp.bfloat16), 'wg').astype(jnp.float32)  15.7 us
  transfers between devices with their start and end apart: 7, of which 7 were waited for; matrix products, arithmetic and copies ran while one was open for 7% of the time, Pallas kernels for 0%

commit v1 on v0

--- a/solution.py
+++ b/solution.py
@@ -1,3 +1,4 @@
+import functools
 import jax
 import jax.numpy as jnp
 from jax import lax
@@ -9,6 +10,21 @@
 ATTEND_CAP = 50.0
 LABEL_CAP = 30.0
 QUERY_SCALE = 1.0 / 12.0
+
+
+def step_on_slot(xin, d0):
+    z1, all_rows = (lax.axis_size("seq"), lax.axis_index("seq"))
+    carry, formed = (xin, 1)
+    while formed < z1:
+        block_next = lax.ppermute(carry, "seq", [(dev_i, dev_i ^ formed) for dev_i in range(z1)])
+        tmp = jnp.concatenate([carry, block_next], axis=d0)
+        next_value = jnp.concatenate([block_next, carry], d0)
+        carry = jnp.where(all_rows & formed == 0, tmp, next_value)
+        formed = 2 * formed
+    return carry
+
+
+assign_the_spans = functools.partial(step_on_slot, d0=0)
 
 
 def rope_tables(positions, head_width):
@@ -68,7 +84,7 @@
     guard_rows = lax.all_to_all(whole_rows, "seq", split_axis=0, concat_axis=0, tiled=True)
     w_query, w_key, w_value, w_out = (
         lax.all_gather(query_weight, "seq", axis=0, tiled=True),
-        lax.all_gather(key_weight, "seq", axis=0, tiled=True),
+        assign_the_spans(key_weight),
         lax.all_gather(value_weight, "seq", axis=0, tiled=True),
         lax.all_gather(out_weight, "seq", axis=1, tiled=True),
     )

time: 378 us -> 360 us (0.952)
  waiting for transfers between devices: 281 us -> 260 us
    ppermute x0 -> x3, waiting for transfers between devices: none -> 115 us  [step_on_slot(): lax.ppermute(carry, 'seq', [(dev_i, dev_i ^ formed) for dev_i in range(z1)])]
    all_gather x1, waiting for transfers between devices: 50 us -> 0.02 us  [shards(): lax.all_gather(value_weight, 'seq', axis=0, tiled=True)]
    all_gather x1, waiting for transfers between devices: 75.5 us -> 39.1 us  [shards(): lax.all_gather(query_weight, 'seq', axis=0, tiled=True)]
    all_gather x1 -> x0, waiting for transfers between devices: 25.5 us -> none  [shards(): lax.all_gather(key_weight, 'seq', axis=0, tiled=True)]
    all_to_all x1, waiting for transfers between devices: 24.1 us -> 0.01 us  [shards(): lax.all_to_all(whole_rows, 'seq', split_axis=0, concat_axis=0, tiled=True)]
    ppermute x0 -> x3, starting transfers between devices: none -> 5.11 us  [step_on_slot(): lax.ppermute(carry, 'seq', [(dev_i, dev_i ^ formed) for dev_i in range(z1)])]
  transfers between devices with their start and end apart: 7 -> 9, of which waited for: 7 -> 6; matrix products, arithmetic and copies ran while one was open for 7% -> 8% of each run, Pallas kernels for 0% -> 0%
where the time goes in v1:
time: 360 us
  waiting for transfers between devices  260 us (72%)
  matrix products  28.9 us (8%)
  blocking collectives  18.7 us (5%)
  local copies, waits for them, and re-layouts  16.4 us (5%)
  between operations  13.7 us (4%)
  other arithmetic  11.8 us (3%)
  starting transfers between devices  10.5 us (3%)
    ppermute x3, waiting for transfers between devices, step_on_slot(): lax.ppermute(carry, 'seq', [(dev_i, dev_i ^ formed) for dev_i in range(z1)])  115 us
    all_gather x1, waiting for transfers between devices, shards(): lax.all_gather(out_weight, 'seq', axis=1, tiled=True)  67.5 us
    all_gather x1, waiting for transfers between devices, shards(): lax.all_gather(query_weight, 'seq', axis=0, tiled=True)  39.1 us
    psum x1, waiting for transfers between devices, shards(): lax.psum(grad_part.astype(jnp.bfloat16), 'wg').astype(jnp.float32)  20.1 us
    all_to_all x1, blocking collectives, shards(): lax.all_to_all(grad_rows.astype(jnp.bfloat16), 'seq', split_axis=0, conca...  16.4 us
    psum x1, waiting for transfers between devices, shards(): lax.psum(out_part.astype(jnp.bfloat16), 'wg').astype(jnp.float32)  15.7 us
    dot_general x5, matrix products, times_transposed(): lax.dot_general(left_side, right_side, (((1,), (1,)), ((), ())), preferre...  8.46 us
  transfers between devices with their start and end apart: 9, of which 6 were waited for; matrix products, arithmetic and copies ran while one was open for 8% of the time, Pallas kernels for 0%

profile of v1, /device:TPU:0, one launch (start us, length us, event | category | flops | bytes accessed | tf_op | source)
XLA Modules:
  0.0 359.5 jit_solution(18335804989358486875)
XLA Ops:
  8.8 3.0 collective-permute-start
  11.8 2.3 all_gather.12
  14.1 5.0 %all-to-all-start = ((bf16[8,16,2304]{2,1,0:T(8,128)(2,1)}), bf16[8,16,2304]{2,1,0:T(8,128)(2,1)S(1)}, u32[]{:S(2)}, u32[]{:S(2)}) async-start(bf16[8,16,2304]{2,1,0:T(8,128)(2,1)} %bitcast), calls=%async_computation | async-start | bytes 1179648 | tf_op jit(solution)/shard_map/all_to_all | solution.py:84
  19.4 2.0 collective-permute-start.1
  23.0 39.3 %collective-permute-done.1 = bf16[576,512]{1,0:T(8,128)(2,1)S(1)} collective-permute-done((bf16[576,512]{1,0:T(8,128)(2,1)S(1)}, bf16[576,512]{1,0:T(8,128)(2,1)S(1)}, u32[]{:S(2)}, u32[]{:S(2)}) %collective-permute-start.1) | collective-permute-done | bytes 589856 | tf_op jit(solution)/shard_map/ppermute | solution.py:19
  63.3 1.0 multiply_convert_fusion.2
  64.3 1.1 bitcast_convert_fusion
  65.5 75.6 %collective-permute-done.2 = bf16[1152,512]{1,0:T(8,128)(2,1)S(1)} collective-permute-done((bf16[1152,512]{1,0:T(8,128)(2,1)S(1)}, bf16[1152,512]{1,0:T(8,128)(2,1)S(1)}, u32[]{:S(2)}, u32[]{:S(2)}) %collective-permute-start.2) | collective-permute-done | bytes 1179680 | tf_op jit(solution)/shard_map/ppermute | solution.py:19
  141.1 1.0 copy-done.7
  142.1 1.8 fusion.35
  143.9 2.8 copy.41
  146.7 1.9 convolution_bitcast_fusion.3
  148.7 2.6 convolution_convert_fusion.3
  151.4 39.1 %all-gather.4.cloned.1.call-done = bf16[2304,1024]{1,0:T(8,128)(2,1)} async-done(((bf16[288,1024]{1,0:T(8,128)(2,1)}), bf16[2304,1024]{1,0:T(8,128)(2,1)}) %all-gather.4.cloned.1.call-update) | async-done | bytes 4718608 | tf_op jit(solution)/shard_map/all_gather | solution.py:86
  190.5 6.8 %copy.12 = bf16[1024,2304]{1,0:T(8,128)(2,1)} copy(bf16[1024,2304]{0,1:T(8,128)(2,1)} %bitcast.103) | data formatting | bytes 9437184 | tf_op jit(solution)/shard_map/dot_general | solution.py:104
  197.3 4.0 %convolution_bitcast_fusion = f32[8,128,128]{1,2,0:T(8,128)S(1)} fusion(bf16[128,2304,1]{1,0,2:T(8,128)(2,1)S(1)} %bitcast.109, bf16[8,128,2304]{2,1,0:T(8,128)(2,1)} %bitcast.106), kind=kOutput, calls=%fused_computation.17 | convolution fusion | flops 603979776 | bytes 5832704 | tf_op jit(solution)/shard_map/dot_general | solution.py:104
  203.3 67.5 %all-gather.8.cloned.1.call-done = bf16[1024,2304]{0,1:T(8,128)(2,1)} async-done(((bf16[1024,288]{0,1:T(8,128)(2,1)}), bf16[1024,2304]{0,1:T(8,128)(2,1)}) %all-gather.8.cloned.1.call-update) | async-done | bytes 4718608 | tf_op jit(solution)/shard_map/all_gather | solution.py:89
  270.8 5.0 %convolution_convert_fusion = bf16[128,2304]{1,0:T(8,128)(2,1)} fusion(bf16[128,1024]{0,1:T(8,128)(2,1)S(1)} %bitcast.118, bf16[1024,2304]{0,1:T(8,128)(2,1)} %all-gather.8.cloned.1.call-done), kind=kOutput, calls=%fused_computation.5 | convolution fusion | flops 604274688 | bytes 5570560 | tf_op jit(solution)/shard_map/dot_general | solution.py:138
  277.2 15.7 %all-reduce.3.cloned.1.call-done = bf16[128,2304]{1,0:T(8,128)(2,1)} async-done(((bf16[128,2304]{1,0:T(8,128)(2,1)}), bf16[128,2304]{1,0:T(8,128)(2,1)}) %all-reduce.3.cloned.1.call-update) | async-done | bytes 589840 | tf_op jit(solution)/shard_map/psum | solution.py:139
  292.9 1.3 fusion.7
  294.2 1.6 multiply_reduce_fusion.2
  297.9 1.1 convolution_convert_fusion.2
  299.1 1.4 fusion.14
  300.8 1.7 convolution_bitcast_fusion.2
  302.5 2.5 convolution_multiply_fusion.1
  305.1 1.2 copy.24
  306.5 4.2 %fusion.68 = f32[128,2304]{1,0:T(8,128)S(1)} fusion(bf16[128,1024]{0,1:T(8,128)(2,1)S(1)} %bitcast.117, bf16[2304,1024]{1,0:T(8,128)(2,1)} %all-gather.4.cloned.1.call-done), kind=kOutput, calls=%fused_computation.126 | convolution fusion | flops 603979776 | bytes 6160384 | tf_op jit(solution)/shard_map/dot_general | solution.py:63
  310.7 0.9 convolution_add_fusion.1
  312.4 1.8 fusion.1
  314.2 20.1 %all-reduce.5.cloned.1.call-done = bf16[128,2304]{1,0:T(8,128)(2,1)} async-done(((bf16[128,2304]{1,0:T(8,128)(2,1)}), bf16[128,2304]{1,0:T(8,128)(2,1)}) %all-reduce.5.cloned.1.call-update) | async-done | bytes 589840 | tf_op jit(solution)/shard_map/psum | solution.py:194
  334.3 1.3 multiply_reduce_fusion
  335.9 16.4 %all_to_all.21 = bf16[8,16,1152]{2,1,0:T(8,128)(2,1)S(1)} all-to-all(bf16[8,16,1152]{2,1,0:T(8,128)(2,1)S(1)} %bitcast.111), channel_id=1, replica_groups=mesh['groups'=2,'seq'=8,'wg'=2] {'seq'}, dimensions={0} | all-to-all | bytes 589824 | tf_op jit(solution)/shard_map/all_to_all | solution.py:199
  (98 shorter events, 12.5 us)
Async XLA Ops:
  6.5 289.3 %copy-start = (bf16[64,2304]{1,0:T(8,128)(2,1)S(1)}, bf16[64,2304]{1,0:T(8,128)(2,1)}, u32[]{:S(2)}) copy-start(bf16[64,2304]{1,0:T(8,128)(2,1)} %param.19) | copy-start | bytes 884740
  6.5 2.2 copy-start.10
  6.5 5.2 %copy-start.9 = (bf16[128,1152]{1,0:T(8,128)(2,1)S(1)}, bf16[128,1152]{1,0:T(8,128)(2,1)}, u32[]{:S(2)}) copy-start(bf16[128,1152]{1,0:T(8,128)(2,1)} %param.11) | copy-start | bytes 884740
  6.5 142.1 %all-gather.6.cloned.1.call-start = ((), (), s32[]{:S(2)}) async-start(), calls=%async_computation.3 | async-start | bytes 2654208 | tf_op jit(solution)/shard_map/all_gather | solution.py:88
  7.3 183.2 %all-gather.4.cloned.1.call-start = ((), (), s32[]{:S(2)}) async-start(), calls=%async_computation.2 | async-start | bytes 5308416 | tf_op jit(solution)/shard_map/all_gather | solution.py:86
  8.0 262.7 %all-gather.8.cloned.1.call-start = ((), (), s32[]{:S(2)}) async-start(), calls=%async_computation.4 | async-start | bytes 5308416 | tf_op jit(solution)/shard_map/all_gather | solution.py:89
  8.8 10.4 %collective-permute-start = (bf16[288,512]{1,0:T(8,128)(2,1)S(1)}, bf16[288,512]{1,0:T(8,128)(2,1)S(1)}, u32[]{:S(2)}, u32[]{:S(2)}) collective-permute-start(bf16[288,512]{1,0:T(8,128)(2,1)S(1)} %copy-done.10), channel_id=1, source_target_pairs={{0,2},{2,0},{4,6},{6,4},{8,10},{10,8},{12,14},{14,12},{1,3},{3,1},... | collective-permute-start | bytes 884744 | tf_op jit(solution)/shard_map/ppermute | solution.py:19
  14.1 7.4 %copy-start.18 = (s32[8]{0:T(128)S(1)}, s32[8]{0:T(128)}, u32[]{:S(2)}) copy-start(s32[8]{0:T(128)} %param.20) | copy-start | bytes 100
  14.1 48.9 %all-to-all-start = ((bf16[8,16,2304]{2,1,0:T(8,128)(2,1)}), bf16[8,16,2304]{2,1,0:T(8,128)(2,1)S(1)}, u32[]{:S(2)}, u32[]{:S(2)}) async-start(bf16[8,16,2304]{2,1,0:T(8,128)(2,1)} %bitcast), calls=%async_computation | async-start | bytes 1179648 | tf_op jit(solution)/shard_map/all_to_all | solution.py:84
  19.1 273.8 %all-reduce.3.cloned.1.call-start = ((), (), s32[]{:S(2)}) async-start(), calls=%async_computation.5 | async-start | bytes 1179648 | tf_op jit(solution)/shard_map/psum | solution.py:139
  19.4 42.9 %collective-permute-start.1 = (bf16[576,512]{1,0:T(8,128)(2,1)S(1)}, bf16[576,512]{1,0:T(8,128)(2,1)S(1)}, u32[]{:S(2)}, u32[]{:S(2)}) collective-permute-start(bf16[576,512]{1,0:T(8,128)(2,1)S(1)} %maximum_select_fusion.2), channel_id=1, source_target_pairs={{0,4},{2,6},{4,0},{6,2},{8,12},{10,14},{12,8},{14,10},{1,5},{3,7},... | collective-permute-start | bytes 1769480 | tf_op jit(solution)/shard_map/ppermute | solution.py:19
  23.0 40.2 %copy-start.13 = (f32[2304]{0:T(1024)S(1)}, f32[2304]{0:T(1024)}, u32[]{:S(2)}) copy-start(f32[2304]{0:T(1024)} %param.12) | copy-start | bytes 27652
  62.9 78.2 %copy-start.5 = (bf16[1152,512]{1,0:T(8,128)(2,1)}, bf16[1152,512]{1,0:T(8,128)(2,1)S(1)}, u32[]{:S(2)}) copy-start(bf16[1152,512]{1,0:T(8,128)(2,1)S(1)} %maximum_select_fusion.1) | copy-start | bytes 3538948
  62.9 78.2 %collective-permute-start.2 = (bf16[1152,512]{1,0:T(8,128)(2,1)S(1)}, bf16[1152,512]{1,0:T(8,128)(2,1)S(1)}, u32[]{:S(2)}, u32[]{:S(2)}) collective-permute-start(bf16[1152,512]{1,0:T(8,128)(2,1)S(1)} %maximum_select_fusion.1), channel_id=1, source_target_pairs={{0,8},{2,10},{4,12},{6,14},{8,0},{10,2},{12,4},{14,6},{1,9},{3,11}... | collective-permute-start | bytes 3538952 | tf_op jit(solution)/shard_map/ppermute | solution.py:19
  141.1 1.0 copy-start.7
  148.6 53.5 %copy-start.15 = (bf16[4,128,64]{1,2,0:T(8,128)(2,1)}, bf16[4,128,64]{1,2,0:T(8,128)(2,1)S(1)}, u32[]{:S(2)}) copy-start(bf16[4,128,64]{1,2,0:T(8,128)(2,1)S(1)} %get-tuple-element.18) | copy-start | bytes 196612
  190.5 6.8 %copy-start.4 = (bf16[8,16,2304]{2,1,0:T(8,128)(2,1)S(1)}, bf16[8,16,2304]{2,1,0:T(8,128)(2,1)}, u32[]{:S(2)}) copy-start(bf16[8,16,2304]{2,1,0:T(8,128)(2,1)} %multiply_convert_fusion.2) | copy-start | bytes 1769476
  202.1 0.7 copy-start.11
  202.5 0.8 copy-start.20
  270.8 5.2 %copy-start.19 = (s32[8]{0:T(128)S(1)}, s32[8]{0:T(128)}, u32[]{:S(2)}) copy-start(s32[8]{0:T(128)} %param.21) | copy-start | bytes 100
  270.8 27.1 %slice-start = ((s8[4718592]{0:T(1024)(128)(4,1)}), s8[524288]{0:T(1024)(128)(4,1)S(1)}, s32[]{:S(2)}) async-start(s8[4718592]{0:T(1024)(128)(4,1)} %bitcast.104), calls=%async_computation.7 | async-start | bytes 1048576
  275.7 18.5 %copy-start.14 = (f32[2304]{0:T(1024)S(1)}, f32[2304]{0:T(1024)}, u32[]{:S(2)}) copy-start(f32[2304]{0:T(1024)} %param.17) | copy-start | bytes 27652
  275.7 20.1 %copy-start.17 = (f32[2304]{0:T(1024)S(1)}, f32[2304]{0:T(1024)}, u32[]{:S(2)}) copy-start(f32[2304]{0:T(1024)} %param.18) | copy-start | bytes 27652
  275.7 58.6 %all-reduce.5.cloned.1.call-start = ((), (), s32[]{:S(2)}) async-start(), calls=%async_computation.6 | async-start | bytes 1179648 | tf_op jit(solution)/shard_map/psum | solution.py:194
  294.2 3.7 %slice-start.1 = ((s8[4718592]{0:T(1024)(128)(4,1)}), s8[4194304]{0:T(1024)(128)(4,1)S(1)}, s32[]{:S(2)}) async-start(s8[4718592]{0:T(1024)(128)(4,1)} %bitcast.104), calls=%async_computation.8 | async-start | bytes 8388608
  296.3 1.1 copy-start.1
  299.1 1.6 copy-start.12
  300.7 1.7 copy-start.16
  306.4 4.2 %copy-start.6 = (bf16[1152,512]{1,0:T(8,128)(2,1)S(1)}, bf16[1152,512]{1,0:T(8,128)(2,1)}, u32[]{:S(2)}) copy-start(bf16[1152,512]{1,0:T(8,128)(2,1)} %copy-done.5) | copy-start | bytes 3538948
  306.4 4.2 %copy-start.8 = (bf16[1152,512]{1,0:T(8,128)(2,1)S(1)}, bf16[1152,512]{1,0:T(8,128)(2,1)}, u32[]{:S(2)}) copy-start(bf16[1152,512]{1,0:T(8,128)(2,1)} %copy-done.7) | copy-start | bytes 3538948
  310.7 1.7 copy-start.2
  314.2 21.5 %copy-start.3 = (f32[128,2304]{1,0:T(8,128)S(1)}, f32[128,2304]{1,0:T(8,128)}, u32[]{:S(2)}) copy-start(f32[128,2304]{1,0:T(8,128)} %bitcast_convert_fusion) | copy-start | bytes 3538948
Sparse Core Ops, SparseCore 0:
  9.5 92.7 all-gather.5
  104.5 85.9 all-gather.3
  192.7 78.0 all-gather.7
  275.9 16.9 all-reduce.2
  314.3 20.0 all-reduce.4
